TPU v7x, 512 devices: a whole 4x4x16 slice. The times are simulated.
512 devices in a mesh: ctx: 16 (over z), head: 32 (over x, y, core).
Axes of the slice: x: 4, y: 4, z: 16, core: 2. Of those that a mesh axis runs over, the one named last changes fastest.
Arguments:
- tokens_in: bfloat16 [4096, 4096], P('ctx', 'head'), may hold values from -6 to 6
- w_qkv: bfloat16 [4096, 32, 384], P(None, 'head'), may hold values from -0.125 to 0.125
- w_out: bfloat16 [32, 128, 4096], P('head'), may hold values from -0.375 to 0.375
- codebook: bfloat16 [32, 512, 128], P('head'), may hold values from -184 to 184
- codes: int32 [32, 4096], P('head', 'ctx'), may hold values from 0 to 511
- reach: int32 [16], P('ctx'), may hold values from 1 to 256, as said below
Outputs:
- mixed: bfloat16 [4096, 4096], P(('ctx', 'head'))
Inputs may be any that keep to these rules, and one draw needn't show every extreme that they name: reach[g] is how many of the last positions of block g - 1 block g sees with exact keys; reach[0] has no effect.
All inputs are finite; a program needn't handle non-finite values.
Results may differ from a plain program's by a relative error of at most 0.015.
Values may be sent and summed in bfloat16 or wider, within the bound.
No kernel may reach another device: no remote copies, remote signals or barrier semaphores. Data moves between devices by JAX's collectives and lax.ppermute only.
A program may use at most 64 MiB of HBM per device.

v0:
```python
import math
import jax
import jax.numpy as jnp
from jax import lax
from jax.sharding import PartitionSpec as P

BLK = 256


def from_behind(block, axis, distance):
    devices = range(lax.axis_size(axis))
    route = [(i - distance, i) for i in devices if i - distance in devices]
    return lax.ppermute(block, axis, route)


def entering(value, axis, combine, identity):
    devices, index = (lax.axis_size(axis), lax.axis_index(axis))
    everything = jax.tree.map(
        lambda part, kind: lax.all_gather(part.astype(kind), axis),
        value,
        (jnp.bfloat16, jnp.bfloat16),
    )
    start = jax.tree.map(
        lambda part, zero: jnp.broadcast_to(jnp.asarray(zero, part.dtype), part.shape),
        value,
        identity,
    )

    def turn(k, before):
        reached = k < index
        new = combine(
            before, jax.tree.map(lambda part, own: part[k].astype(own.dtype), everything, value)
        )
        return jax.tree.map(lambda a, b: jnp.where(reached, a, b), new, before)

    return lax.fori_loop(0, devices, turn, start)


def attend_block(
    queries, keys_win, vals_win, cache_v, cache_c, book, reach_one, prev_flag, block_len, scale
):
    exact = (
        lax.dot_general(
            queries, keys_win, (((1,), (1,)), ((), ())), preferred_element_type=jnp.float32
        )
        * scale
    )
    coded = (
        lax.dot_general(queries, book, (((1,), (1,)), ((), ())), preferred_element_type=jnp.float32)
        * scale
    )
    rows = lax.broadcasted_iota(jnp.int32, exact.shape, 0)
    cols = lax.broadcasted_iota(jnp.int32, exact.shape, 1)
    prev_ok = (cols < block_len) & (cols >= block_len - reach_one) & prev_flag
    curr_ok = (cols >= block_len) & (cols - block_len <= rows)
    allowed = prev_ok | curr_ok
    valid = cache_c > 0.5
    top = jnp.maximum(
        jnp.max(jnp.where(allowed, exact, -jnp.inf), axis=1),
        jnp.max(jnp.where(valid[None, :], coded, -jnp.inf), axis=1),
    )
    probs = jnp.exp(jnp.where(allowed, exact - top[:, None], -jnp.inf))
    weights = jnp.exp(jnp.where(valid[None, :], coded - top[:, None], -jnp.inf))
    numer = jnp.dot(probs.astype(jnp.bfloat16), vals_win, preferred_element_type=jnp.float32)
    numer = numer + jnp.dot(weights, cache_v, precision=lax.Precision.HIGHEST)
    denom = jnp.sum(probs, axis=1) + jnp.dot(weights, cache_c, precision=lax.Precision.HIGHEST)
    return (numer / denom[:, None]).astype(jnp.bfloat16)


def combine(earlier, later):
    return (earlier[0] + later[0], earlier[1] + later[1])


def on_device(tokens_in, w_qkv, w_out, codebook, codes, reach):
    tok_rows = tokens_in.shape[0]
    head_dim = codebook.shape[2]
    num_codes = codebook.shape[1]
    num_blocks = tok_rows // BLK
    scale = 1.0 / math.sqrt(head_dim)
    w_local = w_qkv[:, 0, :]
    projected = jnp.dot(
        lax.all_gather(tokens_in, "head", axis=1, tiled=True),
        w_local,
        preferred_element_type=jnp.float32,
    )
    queries = projected[:, :head_dim].astype(jnp.bfloat16)
    key_vals = projected[:, head_dim:].astype(jnp.bfloat16)
    code_row = codes[0]
    book = codebook[0]
    prev_kv, prev_codes = from_behind((key_vals, code_row), "ctx", 1)
    has_prev = lax.axis_index("ctx") > 0
    code_ids = jnp.arange(num_codes, dtype=jnp.int32)
    onehot_loc = (code_row[:, None] == code_ids[None, :]).astype(jnp.bfloat16)
    local_v = jnp.einsum(
        "ts,td->sd", onehot_loc, key_vals[:, head_dim:], preferred_element_type=jnp.float32
    )
    local_c = jnp.sum(onehot_loc, axis=0, dtype=jnp.float32)
    before_v, before_c = entering(
        (local_v, local_c), "ctx", combine, (jnp.zeros_like(local_v), jnp.zeros_like(local_c))
    )
    ext_kv = jnp.concatenate([prev_kv, key_vals], axis=0)
    ext_codes = jnp.concatenate([prev_codes, code_row], axis=0)
    ext_len = BLK + tok_rows
    positions = jnp.arange(ext_len, dtype=jnp.int32)[:, None]
    thresholds = (jnp.arange(num_blocks, dtype=jnp.int32) + 1) * BLK - reach
    plus = (positions >= BLK) & (positions < thresholds[None, :])
    minus = (positions < BLK) & (positions >= thresholds[None, :]) & has_prev
    signs = (plus.astype(jnp.float32) - minus.astype(jnp.float32)).astype(jnp.bfloat16)
    signed_vals = (signs[:, :, None] * ext_kv[:, None, head_dim:]).reshape(
        ext_len, num_blocks * head_dim
    )
    onehot_ext = (ext_codes[:, None] == code_ids[None, :]).astype(jnp.bfloat16)
    part_v = jnp.einsum(
        "es,ef->sf", onehot_ext, signed_vals, preferred_element_type=jnp.float32
    ).reshape(num_codes, num_blocks, head_dim)
    part_c = jnp.einsum("es,eb->sb", onehot_ext, signs, preferred_element_type=jnp.float32)
    cache_v = before_v + part_v[:, 0, :]
    cache_c = before_c + part_c[:, 0]
    prev_flag = has_prev | (0 > 0)
    pieces_out = attend_block(
        queries,
        ext_kv[:, :head_dim],
        ext_kv[:, head_dim:],
        cache_v,
        cache_c,
        book,
        reach[0],
        prev_flag,
        BLK,
        scale,
    )
    w_proj = w_out[0]
    mixed = lax.psum_scatter(
        jnp.dot(pieces_out, w_proj, preferred_element_type=jnp.float32).astype(jnp.bfloat16),
        "head",
        scatter_dimension=0,
        tiled=True,
    )
    return mixed


def solution(mesh):
    in_specs = (
        P("ctx", "head"),
        P(None, "head", None),
        P("head", None, None),
        P("head", None, None),
        P("head", "ctx"),
        P("ctx"),
    )
    out_specs = P(("ctx", "head"), None)
    return jax.shard_map(
        on_device, mesh=mesh, in_specs=in_specs, out_specs=out_specs, check_vma=False
    )
```

profile of v0, /device:TPU:2, one launch (start us, length us, event | category | flops | bytes accessed | tf_op | source)
XLA Modules:
  0.0 296.4 jit_solution(15039246053632858118)
XLA Ops:
  6.5 0.0 copy-start
  6.5 0.7 all-gather.6.cloned.1.call-update
  7.3 0.0 all-gather.8.cloned.1.call-start
  7.3 67.3 %all-gather.6.cloned.1.call-done = bf16[256,4096]{1,0:T(8,128)(2,1)} async-done(((bf16[256,128]{1,0:T(8,128)(2,1)}), bf16[256,4096]{1,0:T(8,128)(2,1)}) %all-gather.6.cloned.1.call-update) | async-done | bytes 2097168 | tf_op jit(solution)/shard_map/all_gather | solution.py:82
  74.7 2.8 fusion.2
  77.5 0.7 copy-done.1
  78.2 1.1 convolution_convert_fusion.1
  79.3 0.0 all-gather.8.cloned.1.call-update
  79.3 0.0 reduce-scatter.2.cloned.1.call-start
  79.3 3.5 %collective-permute-start.1 = (s32[256]{0:T(256)S(1)}, s32[256]{0:T(256)S(1)}, u32[]{:S(2)}, u32[]{:S(2)}) collective-permute-start(s32[256]{0:T(256)S(1)} %bitcast.40), channel_id=1, source_target_pairs={{0,32},{32,64},{64,96},{96,128},{128,160},{160,192},{192,224},{224... | collective-permute-start | bytes 3080 | tf_op jit(solution)/shard_map/ppermute | solution.py:13
  82.8 0.1 fusion.20
  83.7 29.7 %all-gather.2 = bf16[16,1,512]{2,1,0:T(2,128)(2,1)S(1)} all-gather(bf16[1,1,512]{2,1,0:T(2,128)(2,1)S(1)} %reshape.63), channel_id=3, replica_groups=mesh['ctx'=16,'head'=32] {'ctx'}, dimensions={0}, use_global_device_ids=true | all-gather | bytes 17408 | tf_op jit(solution)/shard_map/all_gather | solution.py:19
  113.3 0.6 copy.9
  114.0 0.0 collective-permute-done.1
  114.0 0.9 slice.25
  114.9 1.8 collective-permute-start
  116.8 0.9 fusion.8
  117.7 2.1 collective-permute-done
  119.8 0.7 copy-done.2
  120.5 2.5 select_reduce_fusion.1
  122.9 29.8 %all-gather.8.cloned.1.call-done = bf16[8192,128]{1,0:T(8,128)(2,1)} async-done(((bf16[512,128]{1,0:T(8,128)(2,1)}), bf16[8192,128]{1,0:T(8,128)(2,1)}) %all-gather.8.cloned.1.call-update) | async-done | bytes 2097168 | tf_op jit(solution)/shard_map/all_gather | solution.py:19
  152.8 28.5 %while.16 = (s32[]{:T(128)}, f32[512,128]{1,0:T(8,128)S(1)}, f32[512]{0:T(512)S(1)}, s32[]{:T(128)}, bf16[16,512,128]{2,1,0:T(8,128)(2,1)}, /*index=5*/bf16[16,512]{1,0:T(8,128)(2,1)}, s32[]{:T(128)}, s32[]{:T(128)}) while((s32[]{:T(128)}, f32[512,128]{1,0:T(8,128)S(1)}, f32[512]{0:T(512)S(1)}, s32[]{:T(128)}, ...), condition=%wide.region_3.4_spmd.clone, body=%wide.region_2.3_spmd.clone.sunk | while | flops 264196 | bytes 664699 | solution.py:36
  152.8 1.0 add_select_fusion.4
  153.8 0.7 dynamic-slice_convert_fusion.2
  154.5 1.0 add_select_fusion.4
  155.6 0.7 dynamic-slice_convert_fusion.2
  156.3 1.0 add_select_fusion.4
  157.4 0.7 dynamic-slice_convert_fusion.2
  158.1 1.0 add_select_fusion.4
  159.1 0.7 dynamic-slice_convert_fusion.2
  159.9 1.0 add_select_fusion.4
  160.9 0.7 dynamic-slice_convert_fusion.2
  161.7 1.0 add_select_fusion.4
  162.7 0.7 dynamic-slice_convert_fusion.2
  163.4 1.0 add_select_fusion.4
  164.5 0.7 dynamic-slice_convert_fusion.2
  165.2 1.0 add_select_fusion.4
  166.3 0.7 dynamic-slice_convert_fusion.2
  167.0 1.0 add_select_fusion.4
  168.0 0.7 dynamic-slice_convert_fusion.2
  168.8 1.0 add_select_fusion.4
  169.8 0.7 dynamic-slice_convert_fusion.2
  170.6 1.0 add_select_fusion.4
  171.6 0.7 dynamic-slice_convert_fusion.2
  172.3 1.0 add_select_fusion.4
  173.4 0.7 dynamic-slice_convert_fusion.2
  174.1 1.0 add_select_fusion.4
  175.2 0.7 dynamic-slice_convert_fusion.2
  175.9 1.0 add_select_fusion.4
  176.9 0.7 dynamic-slice_convert_fusion.2
  177.7 1.0 add_select_fusion.4
  178.7 0.7 dynamic-slice_convert_fusion.2
  179.5 1.0 add_select_fusion.4
  180.5 0.7 dynamic-slice_convert_fusion.2
  181.2 0.7 broadcast_compare_fusion
  181.9 1.3 select_reduce_fusion
  183.1 0.7 max.7
  183.8 1.3 fusion.16
  185.1 1.5 convolution_add_fusion
  186.6 0.6 fusion.15
  187.3 0.6 fusion.14
  187.9 3.7 %convolution_convert_fusion = bf16[256,4096]{1,0:T(8,128)(2,1)} fusion(f32[256,128]{1,0:T(8,128)S(1)} %fusion.15, bf16[1,128,4096]{2,1,0:T(8,128)(2,1)} %param.10, f32[256,512]{1,0:T(8,128)} %get-tuple-element.153, f32[256]{0:T(256)S(1)} %max.7, s32[512]{0:T(512)S(1)} %iota_add_fusion, pred[512]{0:T(512)(128)(4,1)S(1)} %get-tuple-element.156, ...), kind=kOutput, calls=%fused_computation.3 | convolution fusion | flops 304185344 | bytes 4068352 | tf_op jit(solution)/shard_map/dot_general | solution.py:134
  191.6 0.0 reduce-scatter.2.cloned.1.call-update
  191.7 98.2 %reduce-scatter.2.cloned.1.call-done = bf16[8,4096]{1,0:T(8,128)(2,1)} async-done(((bf16[256,4096]{1,0:T(8,128)(2,1)}), bf16[8,4096]{1,0:T(8,128)(2,1)}) %reduce-scatter.2.cloned.1.call-update) | async-done | bytes 65552 | tf_op jit(solution)/shard_map/reduce_scatter | solution.py:133
  (35 shorter events, 0.3 us)
Async XLA Ops:
  6.5 68.1 %copy-start = (bf16[4096,1,384]{2,0,1:T(8,128)(2,1)S(1)}, bf16[4096,1,384]{2,0,1:T(8,128)(2,1)}, u32[]{:S(2)}) copy-start(bf16[4096,1,384]{2,0,1:T(8,128)(2,1)} %param.9) | copy-start | bytes 9437188
  6.5 68.1 %all-gather.6.cloned.1.call-start = ((), (), s32[]{:S(2)}) async-start(), calls=%async_computation.1 | async-start | bytes 2162688 | tf_op jit(solution)/shard_map/all_gather | solution.py:82
  7.3 70.9 %copy-start.4 = (s32[1,256]{1,0:T(1,128)S(1)}, s32[1,256]{1,0:T(1,128)}, u32[]{:S(2)}) copy-start(s32[1,256]{1,0:T(1,128)} %param.12) | copy-start | bytes 3076
  7.3 145.5 %all-gather.8.cloned.1.call-start = ((), (), s32[]{:S(2)}) async-start(), calls=%async_computation.3 | async-start | bytes 2228224 | tf_op jit(solution)/shard_map/all_gather | solution.py:19
  77.5 0.7 copy-start.1
  79.3 210.6 %reduce-scatter.2.cloned.1.call-start = ((), (), s32[]{:S(2)}) async-start(), calls=%async_computation.2 | async-start | bytes 2162688 | tf_op jit(solution)/shard_map/reduce_scatter | solution.py:133
  79.3 34.6 %collective-permute-start.1 = (s32[256]{0:T(256)S(1)}, s32[256]{0:T(256)S(1)}, u32[]{:S(2)}, u32[]{:S(2)}) collective-permute-start(s32[256]{0:T(256)S(1)} %bitcast.40), channel_id=1, source_target_pairs={{0,32},{32,64},{64,96},{96,128},{128,160},{160,192},{192,224},{224... | collective-permute-start | bytes 3080 | tf_op jit(solution)/shard_map/ppermute | solution.py:13
  83.6 30.3 %copy-start.3 = (bf16[512]{0:T(512)(128)(2,1)}, bf16[512]{0:T(512)(128)(2,1)S(1)}, u32[]{:S(2)}) copy-start(bf16[512]{0:T(512)(128)(2,1)S(1)} %subtract_convert_fusion) | copy-start | bytes 3076
  114.0 5.8 %copy-start.5 = (s32[512]{0:T(512)}, s32[512]{0:T(512)S(1)}, u32[]{:S(2)}) copy-start(s32[512]{0:T(512)S(1)} %pad_add_fusion) | copy-start | bytes 6148
  114.9 4.9 %collective-permute-start = (bf16[256,256]{1,0:T(8,128)(2,1)S(1)}, bf16[256,256]{1,0:T(8,128)(2,1)S(1)}, u32[]{:S(2)}, u32[]{:S(2)}) collective-permute-start(bf16[256,256]{1,0:T(8,128)(2,1)S(1)} %slice.25), channel_id=1, source_target_pairs={{0,32},{32,64},{64,96},{96,128},{128,160},{160,192},{192,224},{224... | collective-permute-start | bytes 393224 | tf_op jit(solution)/shard_map/ppermute | solution.py:13
  119.8 0.7 copy-start.2
Sparse Core Ops, SparseCore 0:
  10.4 64.1 all-gather.5
  79.4 73.3 all-gather.7
  191.8 98.0 reduce-scatter.1
where the time goes:
time: 298 us; the launch traced here: 296 us
  waiting for transfers between devices  198 us (66%)
  other arithmetic  31 us (10%)
  blocking collectives  29.7 us (10%)
  matrix products  15 us (5%)
  between operations  13.9 us (5%)
  starting transfers between devices  5.39 us (2%)
    reduce_scatter x1, waiting for transfers between devices, on_device(): lax.psum_scatter(jnp.dot(pieces_out, w_proj, preferred_element_type=jnp.f...  98.2 us
    all_gather x1, waiting for transfers between devices, on_device(): lax.all_gather(tokens_in, 'head', axis=1, tiled=True)  67.3 us
    all_gather x1, waiting for transfers between devices, entering(): lax.all_gather(part.astype(kind), axis)  29.8 us
    all_gather x1, blocking collectives, entering(): lax.all_gather(part.astype(kind), axis)  29.7 us
    select_n x32, other arithmetic, turn(): return jax.tree.map(lambda a, b: jnp.where(reached, a, b), new, before)  16.8 us
    convert_element_type x16, other arithmetic, turn(): part[k].astype(own.dtype)  11.3 us
  transfers between devices with their start and end apart: 5, of which 4 were waited for; matrix products, arithmetic and copies ran while one was open for 2% of the time, Pallas kernels for 0%

commit v1 on v0

--- a/solution.py
+++ b/solution.py
@@ -5,6 +5,12 @@
 from jax.sharding import PartitionSpec as P
 
 BLK = 256
+
+
+def gather_by_exchange(x, axis, dim):
+    peers = lax.axis_size(axis)
+    repeats = [peers if d == dim else 1 for d in range(x.ndim)]
+    return lax.all_to_all(jnp.tile(x, repeats), axis, split_axis=dim, concat_axis=dim, tiled=True)
 
 
 def from_behind(block, axis, distance):
@@ -79,9 +85,7 @@
     scale = 1.0 / math.sqrt(head_dim)
     w_local = w_qkv[:, 0, :]
     projected = jnp.dot(
-        lax.all_gather(tokens_in, "head", axis=1, tiled=True),
-        w_local,
-        preferred_element_type=jnp.float32,
+        gather_by_exchange(tokens_in, "head", 1), w_local, preferred_element_type=jnp.float32
     )
     queries = projected[:, :head_dim].astype(jnp.bfloat16)
     key_vals = projected[:, head_dim:].astype(jnp.bfloat16)

time: 298 us -> 273 us (0.916)
  waiting for transfers between devices: 198 us -> 129 us
  blocking collectives: 29.7 us -> 68.5 us
  local copies, waits for them, and re-layouts: 2.87 us -> 8.39 us
    all_gather x1 -> x0, waiting for transfers between devices: 67.3 us -> none  [on_device(): lax.all_gather(tokens_in, 'head', axis=1, tiled=True)]
    all_to_all x0 -> x1, blocking collectives: none -> 35 us  [gather_by_exchange(): lax.all_to_all(jnp.tile(x, repeats), axis, split_axis=dim, concat_axis=di...]
    all_to_all x0 -> x1, local copies, waits for them, and re-layouts: none -> 4.06 us  [gather_by_exchange(): lax.all_to_all(jnp.tile(x, repeats), axis, split_axis=dim, concat_axis=di...]
    all_gather x1, blocking collectives: 29.7 us -> 33.5 us  [entering(): lax.all_gather(part.astype(kind), axis)]
  transfers between devices with their start and end apart: 5 -> 4, of which waited for: 4 -> 3; matrix products, arithmetic and copies ran while one was open for 2% -> 2% of each run, Pallas kernels for 0% -> 0%
where the time goes in v1:
time: 273 us; the launch traced here: 271 us
  waiting for transfers between devices  129 us (47%)
  blocking collectives  68.5 us (25%)
  other arithmetic  31 us (11%)
  matrix products  15.1 us (6%)
  between operations  14.2 us (5%)
  local copies, waits for them, and re-layouts  8.39 us (3%)
  starting transfers between devices  4.95 us (2%)
    reduce_scatter x1, waiting for transfers between devices, on_device(): lax.psum_scatter(jnp.dot(pieces_out, w_proj, preferred_element_type=jnp.f...  98.5 us
    all_to_all x1, blocking collectives, gather_by_exchange(): lax.all_to_all(jnp.tile(x, repeats), axis, split_axis=dim, concat_axis=di...  35 us
    all_gather x1, blocking collectives, entering(): lax.all_gather(part.astype(kind), axis)  33.5 us
    all_gather x1, waiting for transfers between devices, entering(): lax.all_gather(part.astype(kind), axis)  27.2 us
    select_n x32, other arithmetic, turn(): return jax.tree.map(lambda a, b: jnp.where(reached, a, b), new, before)  16.8 us
    convert_element_type x16, other arithmetic, turn(): part[k].astype(own.dtype)  11.3 us
  transfers between devices with their start and end apart: 4, of which 3 were waited for; matrix products, arithmetic and copies ran while one was open for 2% of the time, Pallas kernels for 0%

profile of v1, /device:TPU:2, one launch (start us, length us, event | category | flops | bytes accessed | tf_op | source)
XLA Modules:
  0.0 271.3 jit_solution(11717946313345919439)
XLA Ops:
  6.5 0.0 copy-start
  6.5 1.5 tile.2
  8.0 35.0 %all_to_all.9 = bf16[256,32,128]{2,0,1:T(8,128)(2,1)} all-to-all(bf16[256,32,128]{2,0,1:T(8,128)(2,1)S(1)} %tile.2), channel_id=1, replica_groups=mesh['ctx'=16,'head'=32] {'head'}, dimensions={1} | all-to-all | bytes 4194304 | tf_op jit(solution)/shard_map/all_to_all | solution.py:13
  43.0 4.1 %copy.8 = bf16[256,32,128]{0,2,1:T(8,128)(2,1)} copy(bf16[256,32,128]{2,0,1:T(8,128)(2,1)} %all_to_all.9) | data formatting | bytes 4194304 | tf_op jit(solution)/shard_map/all_to_all | solution.py:13
  47.1 2.9 %fusion.2 = bf16[256,384]{1,0:T(8,128)(2,1)S(1)} fusion(bf16[256,4096]{0,1:T(8,128)(2,1)} %bitcast.35, bf16[4096,1,384]{2,0,1:T(8,128)(2,1)S(1)} %copy-done), kind=kOutput, calls=%fused_computation.8 | convolution fusion | flops 805404672 | bytes 5439488 | tf_op jit(solution)/shard_map/dot_general | solution.py:87
  50.0 0.7 copy-done.1
  50.7 1.1 convolution_convert_fusion.1
  51.8 0.0 all-gather.5.cloned.1.call-update
  51.8 0.0 reduce-scatter.2.cloned.1.call-start
  51.9 2.0 collective-permute-start.1
  54.5 0.1 fusion.20
  54.7 33.5 %all-gather.2 = bf16[16,1,512]{2,1,0:T(2,128)(2,1)S(1)} all-gather(bf16[1,1,512]{2,1,0:T(2,128)(2,1)S(1)} %reshape.70), channel_id=3, replica_groups=mesh['ctx'=16,'head'=32] {'ctx'}, dimensions={0}, use_global_device_ids=true | all-gather | bytes 17408 | tf_op jit(solution)/shard_map/all_gather | solution.py:25
  88.2 0.6 copy.11
  88.8 0.0 collective-permute-done.1
  88.8 0.9 slice.25
  89.7 2.9 %collective-permute-start = (bf16[256,256]{1,0:T(8,128)(2,1)S(1)}, bf16[256,256]{1,0:T(8,128)(2,1)S(1)}, u32[]{:S(2)}, u32[]{:S(2)}) collective-permute-start(bf16[256,256]{1,0:T(8,128)(2,1)S(1)} %slice.25), channel_id=1, source_target_pairs={{0,32},{32,64},{64,96},{96,128},{128,160},{160,192},{192,224},{224... | collective-permute-start | bytes 393224 | tf_op jit(solution)/shard_map/ppermute | solution.py:19
  92.7 0.9 fusion.8
  93.6 3.1 %collective-permute-done = bf16[256,256]{1,0:T(8,128)(2,1)S(1)} collective-permute-done((bf16[256,256]{1,0:T(8,128)(2,1)S(1)}, bf16[256,256]{1,0:T(8,128)(2,1)S(1)}, u32[]{:S(2)}, u32[]{:S(2)}) %collective-permute-start) | collective-permute-done | bytes 131104 | tf_op jit(solution)/shard_map/ppermute | solution.py:19
  96.7 0.6 copy-done.2
  97.4 2.5 select_reduce_fusion.1
  99.8 27.2 %all-gather.5.cloned.1.call-done = bf16[8192,128]{1,0:T(8,128)(2,1)} async-done(((bf16[512,128]{1,0:T(8,128)(2,1)}), bf16[8192,128]{1,0:T(8,128)(2,1)}) %all-gather.5.cloned.1.call-update) | async-done | bytes 2097168 | tf_op jit(solution)/shard_map/all_gather | solution.py:25
  127.0 28.5 %while.16 = (s32[]{:T(128)}, f32[512,128]{1,0:T(8,128)S(1)}, f32[512]{0:T(512)S(1)}, s32[]{:T(128)}, bf16[16,512,128]{2,1,0:T(8,128)(2,1)}, /*index=5*/bf16[16,512]{1,0:T(8,128)(2,1)}, s32[]{:T(128)}, s32[]{:T(128)}) while((s32[]{:T(128)}, f32[512,128]{1,0:T(8,128)S(1)}, f32[512]{0:T(512)S(1)}, s32[]{:T(128)}, ...), condition=%wide.region_3.4_spmd.clone, body=%wide.region_2.3_spmd.clone.sunk | while | flops 264196 | bytes 664691 | solution.py:42
  127.0 1.0 add_select_fusion.4
  128.1 0.7 dynamic-slice_convert_fusion.2
  128.8 1.0 add_select_fusion.4
  129.9 0.7 dynamic-slice_convert_fusion.2
  130.6 1.0 add_select_fusion.4
  131.6 0.7 dynamic-slice_convert_fusion.2
  132.4 1.0 add_select_fusion.4
  133.4 0.7 dynamic-slice_convert_fusion.2
  134.2 1.0 add_select_fusion.4
  135.2 0.7 dynamic-slice_convert_fusion.2
  135.9 1.0 add_select_fusion.4
  137.0 0.7 dynamic-slice_convert_fusion.2
  137.7 1.0 add_select_fusion.4
  138.8 0.7 dynamic-slice_convert_fusion.2
  139.5 1.0 add_select_fusion.4
  140.5 0.7 dynamic-slice_convert_fusion.2
  141.3 1.0 add_select_fusion.4
  142.3 0.7 dynamic-slice_convert_fusion.2
  143.1 1.0 add_select_fusion.4
  144.1 0.7 dynamic-slice_convert_fusion.2
  144.8 1.0 add_select_fusion.4
  145.9 0.7 dynamic-slice_convert_fusion.2
  146.6 1.0 add_select_fusion.4
  147.7 0.7 dynamic-slice_convert_fusion.2
  148.4 1.0 add_select_fusion.4
  149.4 0.7 dynamic-slice_convert_fusion.2
  150.2 1.0 add_select_fusion.4
  151.2 0.7 dynamic-slice_convert_fusion.2
  152.0 1.0 add_select_fusion.4
  153.0 0.7 dynamic-slice_convert_fusion.2
  153.7 1.0 add_select_fusion.4
  154.8 0.7 dynamic-slice_convert_fusion.2
  155.5 0.7 broadcast_compare_fusion
  156.2 1.3 select_reduce_fusion
  157.5 0.7 max.7
  158.1 1.3 fusion.16
  159.5 0.6 fusion.14
  160.1 1.5 convolution_add_fusion
  161.6 0.6 fusion.15
  162.2 3.7 %convolution_convert_fusion = bf16[256,4096]{1,0:T(8,128)(2,1)} fusion(f32[256,128]{1,0:T(8,128)S(1)} %fusion.15, bf16[1,128,4096]{2,1,0:T(8,128)(2,1)} %param.10, f32[256,512]{1,0:T(8,128)} %get-tuple-element.153, f32[256]{0:T(256)S(1)} %max.7, s32[512]{0:T(512)S(1)} %iota_add_fusion, pred[512]{0:T(512)(128)(4,1)S(1)} %get-tuple-element.156, ...), kind=kOutput, calls=%fused_computation.3 | convolution fusion | flops 304185344 | bytes 4068352 | tf_op jit(solution)/shard_map/dot_general | solution.py:138
  166.0 0.0 reduce-scatter.2.cloned.1.call-update
  166.0 98.5 %reduce-scatter.2.cloned.1.call-done = bf16[8,4096]{1,0:T(8,128)(2,1)} async-done(((bf16[256,4096]{1,0:T(8,128)(2,1)}), bf16[8,4096]{1,0:T(8,128)(2,1)}) %reduce-scatter.2.cloned.1.call-update) | async-done | bytes 65552 | tf_op jit(solution)/shard_map/reduce_scatter | solution.py:137
  (35 shorter events, 0.3 us)
Async XLA Ops:
  6.5 40.6 %copy-start = (bf16[4096,1,384]{2,0,1:T(8,128)(2,1)S(1)}, bf16[4096,1,384]{2,0,1:T(8,128)(2,1)}, u32[]{:S(2)}) copy-start(bf16[4096,1,384]{2,0,1:T(8,128)(2,1)} %param.9) | copy-start | bytes 9437188
  6.5 120.5 %all-gather.5.cloned.1.call-start = ((), (), s32[]{:S(2)}) async-start(), calls=%async_computation.3 | async-start | bytes 2228224 | tf_op jit(solution)/shard_map/all_gather | solution.py:25
  47.1 3.6 %copy-start.4 = (s32[1,256]{1,0:T(1,128)S(1)}, s32[1,256]{1,0:T(1,128)}, u32[]{:S(2)}) copy-start(s32[1,256]{1,0:T(1,128)} %param.12) | copy-start | bytes 3076
  50.0 0.7 copy-start.1
  51.8 212.7 %reduce-scatter.2.cloned.1.call-start = ((), (), s32[]{:S(2)}) async-start(), calls=%async_computation.2 | async-start | bytes 2162688 | tf_op jit(solution)/shard_map/reduce_scatter | solution.py:137
  51.9 36.9 %collective-permute-start.1 = (s32[256]{0:T(256)S(1)}, s32[256]{0:T(256)S(1)}, u32[]{:S(2)}, u32[]{:S(2)}) collective-permute-start(s32[256]{0:T(256)S(1)} %bitcast.42), channel_id=1, source_target_pairs={{0,32},{32,64},{64,96},{96,128},{128,160},{160,192},{192,224},{224... | collective-permute-start | bytes 3080 | tf_op jit(solution)/shard_map/ppermute | solution.py:19
  54.7 34.1 %copy-start.3 = (bf16[512]{0:T(512)(128)(2,1)}, bf16[512]{0:T(512)(128)(2,1)S(1)}, u32[]{:S(2)}) copy-start(bf16[512]{0:T(512)(128)(2,1)S(1)} %subtract_convert_fusion) | copy-start | bytes 3076
  88.8 7.9 %copy-start.5 = (s32[512]{0:T(512)}, s32[512]{0:T(512)S(1)}, u32[]{:S(2)}) copy-start(s32[512]{0:T(512)S(1)} %pad_add_fusion) | copy-start | bytes 6148
  89.7 7.0 %collective-permute-start = (bf16[256,256]{1,0:T(8,128)(2,1)S(1)}, bf16[256,256]{1,0:T(8,128)(2,1)S(1)}, u32[]{:S(2)}, u32[]{:S(2)}) collective-permute-start(bf16[256,256]{1,0:T(8,128)(2,1)S(1)} %slice.25), channel_id=1, source_target_pairs={{0,32},{32,64},{64,96},{96,128},{128,160},{160,192},{192,224},{224... | collective-permute-start | bytes 393224 | tf_op jit(solution)/shard_map/ppermute | solution.py:19
  96.7 0.6 copy-start.2
Sparse Core Ops, SparseCore 0:
  51.9 75.0 all-gather.4
  166.1 98.3 reduce-scatter.1
